TPU v7x, 32 devices: a whole 2x2x4 slice. The times are simulated.
32 devices in a mesh: grp: 2 (over x), row: 16 (over z, y, core).
Axes of the slice: x: 2, y: 2, z: 4, core: 2. Of those that a mesh axis runs over, the one named last changes fastest.
Arguments:
- panels: bfloat16 [3, 8192, 1536], P(None, 'row'), may hold values from -0.099436891 to 0.099436891, as said below
- first_f: bfloat16 [1536, 512], P('row', 'grp'), parts along dimension 1, may hold values from -6 to 6
- first_g: bfloat16 [1536, 512], P('row', 'grp'), parts along dimension 1, may hold values from -6 to 6
- phase: float32 [4, 1536], P('grp'), parts along dimension 0, may hold values from -3.140625 to 3.140625
- wavenum: float32 [4, 1536], P('grp'), parts along dimension 0, may hold values from 0.5 to 2
Outputs:
- final_f: float32 [1536, 512], P('row', 'grp'), parts along dimension 1
- final_g: float32 [1536, 512], P('row', 'grp'), parts along dimension 1
There are 2 independent parts, one for each index of `grp`. A program takes and returns all parts, laid end to end along the dimension named above; an argument that names none is the same for every part. Nothing has to cross between parts.
Inputs may be any that keep to these rules, and one draw needn't show every extreme that they name: `panels`: consecutive sectors' surface functions share part of their shape.
All inputs are finite; a program needn't handle non-finite values.
Results may differ from a plain program's by a relative error of at most 0.013.
Values may be sent and summed in bfloat16 or wider, within the bound.
No kernel may reach another device: no remote copies, remote signals or barrier semaphores. Data moves between devices by JAX's collectives and lax.ppermute only.
A program may use at most 64 MiB of HBM per device.

v0:
```python
import jax
import jax.numpy as jnp
from jax import lax
from jax.sharding import PartitionSpec as P

SECTORS = 2


def contract_rows(left, right):
    return lax.dot_general(
        left, right, (((0,), (0,)), ((), ())), preferred_element_type=jnp.float32
    )


def shards(panels, first_f, first_g, phase, wavenum):
    chan_rows = first_f.shape[0]
    width = first_f.shape[1]
    all_channels = chan_rows * lax.axis_size("row")
    first_row = lax.axis_index("row") * chan_rows
    state = jnp.concatenate([first_f, first_g], axis=1).astype(jnp.float32)
    for sector in range(SECTORS):
        current = panels[sector]
        following = panels[sector + 1]
        solutions = state.astype(jnp.bfloat16)
        flipped = lax.psum_scatter(
            contract_rows(following, current), "row", scatter_dimension=0, tiled=True
        ).astype(jnp.bfloat16)
        rotated = jnp.dot(
            flipped,
            lax.all_gather(solutions, "row", axis=0, tiled=True),
            preferred_element_type=jnp.float32,
        )
        rot_amp = rotated[:, :width]
        rot_der = rotated[:, width:]
        angle_rows = lax.dynamic_slice_in_dim(phase[sector], first_row, chan_rows, 0)
        wave_rows = lax.dynamic_slice_in_dim(wavenum[sector], first_row, chan_rows, 0)
        cosine = jnp.cos(angle_rows)[:, None]
        sine = jnp.sin(angle_rows)[:, None]
        wave = wave_rows[:, None]
        new_amp = cosine * rot_amp + sine / wave * rot_der
        new_der = -wave * sine * rot_amp + cosine * rot_der
        local_norm = jnp.sum(new_amp * new_amp, axis=0) + jnp.sum(new_der * new_der, axis=0)
        norm = lax.psum(local_norm, "row")
        scale = 1.0 / jnp.sqrt(norm / (2.0 * all_channels) + 1e-06)
        state = jnp.concatenate([new_amp * scale[None, :], new_der * scale[None, :]], axis=1)
    return (state[:, :width], state[:, width:])


def solution(mesh):
    in_specs = (
        P(None, "row", None),
        P("row", "grp"),
        P("row", "grp"),
        P("grp", None),
        P("grp", None),
    )
    out_specs = (P("row", "grp"), P("row", "grp"))
    return jax.shard_map(shards, mesh=mesh, in_specs=in_specs, out_specs=out_specs, check_vma=False)
```

profile of v0, /device:TPU:0, one launch (start us, length us, event | category | flops | bytes accessed | tf_op | source)
XLA Modules:
  0.0 366.6 jit_solution(17294964851320102471)
XLA Ops:
  7.2 0.0 all-gather.3.cloned.1.call-start
  7.2 1.5 pad_maximum_fusion
  8.7 0.0 all-gather.3.cloned.1.call-update
  8.7 0.0 reduce-scatter.5.cloned.1.call-start
  8.8 8.2 %fusion = f32[1536,1536]{1,0:T(8,128)} fusion(bf16[3,512,1536]{2,1,0:T(8,128)(2,1)} %param.5), kind=kOutput, calls=%fused_computation | convolution fusion | flops 2415919104 | bytes 12582912 | tf_op jit(solution)/shard_map/dot_general | solution.py:10
  16.9 0.0 reduce-scatter.5.cloned.1.call-update
  17.0 0.0 reduce-scatter.3.cloned.1.call-start
  17.0 8.2 %fusion.3 = f32[1536,1536]{1,0:T(8,128)} fusion(bf16[3,512,1536]{2,1,0:T(8,128)(2,1)} %param.5), kind=kOutput, calls=%fused_computation.3 | convolution fusion | flops 2415919104 | bytes 12582912 | tf_op jit(solution)/shard_map/dot_general | solution.py:10
  25.2 0.0 copy-start
  25.2 0.0 copy-start.1
  25.2 0.0 reduce-scatter.3.cloned.1.call-update
  25.2 0.0 all-gather.5.cloned.1.call-start
  25.3 0.6 copy-done
  25.9 0.0 copy-done.1
  25.9 0.1 cosine_bitcast_fusion
  26.0 0.1 bitcast_divide_fusion.1
  26.2 27.1 %all-gather.3.cloned.1.call-done = bf16[1536,512]{1,0:T(8,128)(2,1)} async-done(((bf16[96,512]{1,0:T(8,128)(2,1)}), bf16[1536,512]{1,0:T(8,128)(2,1)}) %all-gather.3.cloned.1.call-update) | async-done | bytes 1572880 | tf_op jit(solution)/shard_map/all_gather | solution.py:30
  53.3 114.4 %reduce-scatter.5.cloned.1.call-done = f32[96,1536]{1,0:T(8,128)} async-done(((f32[1536,1536]{1,0:T(8,128)}), f32[96,1536]{1,0:T(8,128)}) %reduce-scatter.5.cloned.1.call-update) | async-done | bytes 589840 | tf_op jit(solution)/shard_map/reduce_scatter | solution.py:25
  167.6 2.0 fusion.10
  169.6 0.1 multiply_reduce_fusion.2
  169.7 32.2 %psum.14 = f32[256]{0:T(256)S(1)} all-reduce(f32[256]{0:T(256)S(1)} %add.41), channel_id=1, replica_groups=mesh['grp'=2,'row'=16] {'row'}, use_global_device_ids=true, to_apply=%region_4.0 | all-reduce | flops 256 | bytes 2048 | tf_op jit(solution)/shard_map/psum | solution.py:43
  202.0 0.1 multiply_convert_fusion.1
  202.1 0.6 pad_maximum_fusion.1
  202.7 0.0 all-gather.5.cloned.1.call-update
  202.8 0.1 cosine_bitcast_fusion.1
  202.9 0.1 bitcast_divide_fusion
  203.0 80.4 %reduce-scatter.3.cloned.1.call-done = f32[96,1536]{1,0:T(8,128)} async-done(((f32[1536,1536]{1,0:T(8,128)}), f32[96,1536]{1,0:T(8,128)}) %reduce-scatter.3.cloned.1.call-update) | async-done | bytes 589840 | tf_op jit(solution)/shard_map/reduce_scatter | solution.py:25
  283.4 42.2 %all-gather.5.cloned.1.call-done = bf16[1536,512]{1,0:T(8,128)(2,1)} async-done(((bf16[96,512]{1,0:T(8,128)(2,1)}), bf16[1536,512]{1,0:T(8,128)(2,1)}) %all-gather.5.cloned.1.call-update) | async-done | bytes 1572880 | tf_op jit(solution)/shard_map/all_gather | solution.py:30
  325.6 2.0 fusion.12
  327.6 0.1 multiply_reduce_fusion
  327.7 31.6 %psum.15 = f32[256]{0:T(256)S(1)} all-reduce(f32[256]{0:T(256)S(1)} %add.45), channel_id=1, replica_groups=mesh['grp'=2,'row'=16] {'row'}, use_global_device_ids=true, to_apply=%region_7.0 | all-reduce | flops 256 | bytes 2048 | tf_op jit(solution)/shard_map/psum | solution.py:43
  359.3 0.8 broadcast_multiply_fusion
  (5 shorter events, 0.0 us)
Async XLA Ops:
  7.2 46.1 %all-gather.3.cloned.1.call-start = ((), (), s32[]{:S(2)}) async-start(), calls=%async_computation.4 | async-start | bytes 1671168 | tf_op jit(solution)/shard_map/all_gather | solution.py:30
  8.7 158.9 %reduce-scatter.5.cloned.1.call-start = ((), (), s32[]{:S(2)}) async-start(), calls=%async_computation.3 | async-start | bytes 10027008 | tf_op jit(solution)/shard_map/reduce_scatter | solution.py:25
  17.0 266.4 %reduce-scatter.3.cloned.1.call-start = ((), (), s32[]{:S(2)}) async-start(), calls=%async_computation.2 | async-start | bytes 10027008 | tf_op jit(solution)/shard_map/reduce_scatter | solution.py:25
  25.2 0.7 copy-start
  25.2 0.7 copy-start.1
  25.2 300.4 %all-gather.5.cloned.1.call-start = ((), (), s32[]{:S(2)}) async-start(), calls=%async_computation.5 | async-start | bytes 1671168 | tf_op jit(solution)/shard_map/all_gather | solution.py:30
Sparse Core Ops, SparseCore 0:
  10.9 42.3 all-gather.2
  57.4 110.2 reduce-scatter.4
  172.3 111.0 reduce-scatter.2
  286.1 39.4 all-gather.4
where the time goes:
time: 367 us
  waiting for transfers between devices  264 us (72%)
  blocking collectives  63.8 us (17%)
  matrix products  20.3 us (6%)
  between operations  13.8 us (4%)
    reduce_scatter x2, waiting for transfers between devices, shards(): lax.psum_scatter(contract_rows(following, current), 'row', scatter_dimens...  195 us
    all_gather x2, waiting for transfers between devices, shards(): lax.all_gather(solutions, 'row', axis=0, tiled=True)  69.3 us
    psum x2, blocking collectives, shards(): norm = lax.psum(local_norm, 'row')  63.8 us
    dot_general x2, matrix products, contract_rows(): lax.dot_general(left, right, (((0,), (0,)), ((), ())), preferred_element_...  16.3 us
  transfers between devices with their start and end apart: 4, of which 4 were waited for; matrix products, arithmetic and copies ran while one was open for 5% of the time, Pallas kernels for 0%

commit v1 on v0

--- a/solution.py
+++ b/solution.py
@@ -4,6 +4,18 @@
 from jax.sharding import PartitionSpec as P
 
 SECTORS = 2
+
+
+def gather_around(shard, axis, dim):
+    ways, here, lap = (lax.axis_size(axis), lax.axis_index(axis), shard.shape[dim])
+    shape = [n * ways if d == dim else n for d, n in enumerate(shard.shape)]
+    full = lax.dynamic_update_slice_in_dim(
+        jnp.zeros(shape, shard.dtype), shard, here * lap, axis=dim
+    )
+    for far in range(1, ways):
+        shard = lax.ppermute(shard, axis, [(d, (d + 1) % ways) for d in range(ways)])
+        full = lax.dynamic_update_slice_in_dim(full, shard, (here - far) % ways * lap, axis=dim)
+    return full
 
 
 def contract_rows(left, right):
@@ -26,9 +38,7 @@
             contract_rows(following, current), "row", scatter_dimension=0, tiled=True
         ).astype(jnp.bfloat16)
         rotated = jnp.dot(
-            flipped,
-            lax.all_gather(solutions, "row", axis=0, tiled=True),
-            preferred_element_type=jnp.float32,
+            flipped, gather_around(solutions, "row", 0), preferred_element_type=jnp.float32
         )
         rot_amp = rotated[:, :width]
         rot_der = rotated[:, width:]

time: 367 us -> 330 us (0.90)
  waiting for transfers between devices: 264 us -> 233 us
  blocking collectives: 63.8 us -> 59 us
    ppermute x0 -> x30, waiting for transfers between devices: none -> 233 us  [gather_around(): lax.ppermute(shard, axis, [(d, (d + 1) % ways) for d in range(ways)])]
    reduce_scatter x2, waiting for transfers between devices: 195 us -> 0.04 us  [shards(): lax.psum_scatter(contract_rows(following, current), 'row', scatter_dimens...]
    all_gather x2 -> x0, waiting for transfers between devices: 69.3 us -> none  [shards(): lax.all_gather(solutions, 'row', axis=0, tiled=True)]
    psum x2, blocking collectives: 63.8 us -> 59 us  [shards(): norm = lax.psum(local_norm, 'row')]
  transfers between devices with their start and end apart: 4 -> 32, of which waited for: 4 -> 30; matrix products, arithmetic and copies ran while one was open for 5% -> 3% of each run, Pallas kernels for 0% -> 0%
where the time goes in v1:
time: 330 us
  waiting for transfers between devices  233 us (71%)
  blocking collectives  59 us (18%)
  matrix products  19.3 us (6%)
  between operations  14.3 us (4%)
    ppermute x30, waiting for transfers between devices, gather_around(): lax.ppermute(shard, axis, [(d, (d + 1) % ways) for d in range(ways)])  233 us
    psum x2, blocking collectives, shards(): norm = lax.psum(local_norm, 'row')  59 us
    dot_general x2, matrix products, contract_rows(): lax.dot_general(left, right, (((0,), (0,)), ((), ())), preferred_element_...  16.4 us
  transfers between devices with their start and end apart: 32, of which 30 were waited for; matrix products, arithmetic and copies ran while one was open for 3% of the time, Pallas kernels for 0%

profile of v1, /device:TPU:0, one launch (start us, length us, event | category | flops | bytes accessed | tf_op | source)
XLA Modules:
  0.0 329.7 jit_solution(10051215555196242639)
XLA Ops:
  7.2 0.0 reduce-scatter.5.cloned.1.call-start
  7.2 8.2 %fusion = f32[1536,1536]{1,0:T(8,128)} fusion(bf16[3,512,1536]{2,1,0:T(8,128)(2,1)} %param.5), kind=kOutput, calls=%fused_computation | convolution fusion | flops 2415919104 | bytes 12582912 | tf_op jit(solution)/shard_map/dot_general | solution.py:22
  15.4 0.0 reduce-scatter.5.cloned.1.call-update
  15.5 0.0 reduce-scatter.3.cloned.1.call-start
  15.5 8.2 %fusion.3 = f32[1536,1536]{1,0:T(8,128)} fusion(bf16[3,512,1536]{2,1,0:T(8,128)(2,1)} %param.5), kind=kOutput, calls=%fused_computation.3 | convolution fusion | flops 2415919104 | bytes 12582912 | tf_op jit(solution)/shard_map/dot_general | solution.py:22
  23.7 0.0 reduce-scatter.3.cloned.1.call-update
  23.7 0.8 copy-done
  24.5 0.0 copy-done.1
  24.5 0.5 collective-permute-start
  25.0 0.1 bitcast_divide_fusion.1
  25.1 0.1 bitcast_divide_fusion
  25.3 0.1 broadcast.29.clone
  25.4 0.1 cosine_bitcast_fusion
  25.5 6.8 %collective-permute-done = bf16[96,512]{1,0:T(8,128)(2,1)S(1)} collective-permute-done((bf16[96,512]{1,0:T(8,128)(2,1)S(1)}, bf16[96,512]{1,0:T(8,128)(2,1)S(1)}, u32[]{:S(2)}, u32[]{:S(2)}) %collective-permute-start) | collective-permute-done | bytes 98336 | tf_op jit(solution)/shard_map/ppermute | solution.py:16
  32.3 0.0 collective-permute-start.1
  32.3 6.7 %collective-permute-done.1 = bf16[96,512]{1,0:T(8,128)(2,1)S(1)} collective-permute-done((bf16[96,512]{1,0:T(8,128)(2,1)S(1)}, bf16[96,512]{1,0:T(8,128)(2,1)S(1)}, u32[]{:S(2)}, u32[]{:S(2)}) %collective-permute-start.1) | collective-permute-done | bytes 98336 | tf_op jit(solution)/shard_map/ppermute | solution.py:16
  39.1 6.7 %collective-permute-done.2 = bf16[96,512]{1,0:T(8,128)(2,1)S(1)} collective-permute-done((bf16[96,512]{1,0:T(8,128)(2,1)S(1)}, bf16[96,512]{1,0:T(8,128)(2,1)S(1)}, u32[]{:S(2)}, u32[]{:S(2)}) %collective-permute-start.2) | collective-permute-done | bytes 98336 | tf_op jit(solution)/shard_map/ppermute | solution.py:16
  45.8 0.0 collective-permute-start.3
  45.8 6.7 %collective-permute-done.3 = bf16[96,512]{1,0:T(8,128)(2,1)S(1)} collective-permute-done((bf16[96,512]{1,0:T(8,128)(2,1)S(1)}, bf16[96,512]{1,0:T(8,128)(2,1)S(1)}, u32[]{:S(2)}, u32[]{:S(2)}) %collective-permute-start.3) | collective-permute-done | bytes 98336 | tf_op jit(solution)/shard_map/ppermute | solution.py:16
  52.5 0.0 collective-permute-start.4
  52.5 8.8 %collective-permute-done.4 = bf16[96,512]{1,0:T(8,128)(2,1)S(1)} collective-permute-done((bf16[96,512]{1,0:T(8,128)(2,1)S(1)}, bf16[96,512]{1,0:T(8,128)(2,1)S(1)}, u32[]{:S(2)}, u32[]{:S(2)}) %collective-permute-start.4) | collective-permute-done | bytes 98336 | tf_op jit(solution)/shard_map/ppermute | solution.py:16
  61.3 0.0 collective-permute-start.5
  61.4 8.8 %collective-permute-done.5 = bf16[96,512]{1,0:T(8,128)(2,1)S(1)} collective-permute-done((bf16[96,512]{1,0:T(8,128)(2,1)S(1)}, bf16[96,512]{1,0:T(8,128)(2,1)S(1)}, u32[]{:S(2)}, u32[]{:S(2)}) %collective-permute-start.5) | collective-permute-done | bytes 98336 | tf_op jit(solution)/shard_map/ppermute | solution.py:16
  70.2 0.0 collective-permute-start.6
  70.2 9.0 %collective-permute-done.6 = bf16[96,512]{1,0:T(8,128)(2,1)S(1)} collective-permute-done((bf16[96,512]{1,0:T(8,128)(2,1)S(1)}, bf16[96,512]{1,0:T(8,128)(2,1)S(1)}, u32[]{:S(2)}, u32[]{:S(2)}) %collective-permute-start.6) | collective-permute-done | bytes 98336 | tf_op jit(solution)/shard_map/ppermute | solution.py:16
  79.2 9.0 %collective-permute-done.7 = bf16[96,512]{1,0:T(8,128)(2,1)S(1)} collective-permute-done((bf16[96,512]{1,0:T(8,128)(2,1)S(1)}, bf16[96,512]{1,0:T(8,128)(2,1)S(1)}, u32[]{:S(2)}, u32[]{:S(2)}) %collective-permute-start.7) | collective-permute-done | bytes 98336 | tf_op jit(solution)/shard_map/ppermute | solution.py:16
  88.3 9.0 %collective-permute-done.8 = bf16[96,512]{1,0:T(8,128)(2,1)S(1)} collective-permute-done((bf16[96,512]{1,0:T(8,128)(2,1)S(1)}, bf16[96,512]{1,0:T(8,128)(2,1)S(1)}, u32[]{:S(2)}, u32[]{:S(2)}) %collective-permute-start.8) | collective-permute-done | bytes 98336 | tf_op jit(solution)/shard_map/ppermute | solution.py:16
  97.3 6.8 %collective-permute-done.9 = bf16[96,512]{1,0:T(8,128)(2,1)S(1)} collective-permute-done((bf16[96,512]{1,0:T(8,128)(2,1)S(1)}, bf16[96,512]{1,0:T(8,128)(2,1)S(1)}, u32[]{:S(2)}, u32[]{:S(2)}) %collective-permute-start.9) | collective-permute-done | bytes 98336 | tf_op jit(solution)/shard_map/ppermute | solution.py:16
  104.1 0.0 collective-permute-start.10
  104.1 6.7 %collective-permute-done.10 = bf16[96,512]{1,0:T(8,128)(2,1)S(1)} collective-permute-done((bf16[96,512]{1,0:T(8,128)(2,1)S(1)}, bf16[96,512]{1,0:T(8,128)(2,1)S(1)}, u32[]{:S(2)}, u32[]{:S(2)}) %collective-permute-start.10) | collective-permute-done | bytes 98336 | tf_op jit(solution)/shard_map/ppermute | solution.py:16
  110.9 0.0 collective-permute-start.11
  110.9 6.9 %collective-permute-done.11 = bf16[96,512]{1,0:T(8,128)(2,1)S(1)} collective-permute-done((bf16[96,512]{1,0:T(8,128)(2,1)S(1)}, bf16[96,512]{1,0:T(8,128)(2,1)S(1)}, u32[]{:S(2)}, u32[]{:S(2)}) %collective-permute-start.11) | collective-permute-done | bytes 98336 | tf_op jit(solution)/shard_map/ppermute | solution.py:16
  117.8 0.0 collective-permute-start.12
  117.8 8.9 %collective-permute-done.12 = bf16[96,512]{1,0:T(8,128)(2,1)S(1)} collective-permute-done((bf16[96,512]{1,0:T(8,128)(2,1)S(1)}, bf16[96,512]{1,0:T(8,128)(2,1)S(1)}, u32[]{:S(2)}, u32[]{:S(2)}) %collective-permute-start.12) | collective-permute-done | bytes 98336 | tf_op jit(solution)/shard_map/ppermute | solution.py:16
  126.7 9.0 %collective-permute-done.13 = bf16[96,512]{1,0:T(8,128)(2,1)S(1)} collective-permute-done((bf16[96,512]{1,0:T(8,128)(2,1)S(1)}, bf16[96,512]{1,0:T(8,128)(2,1)S(1)}, u32[]{:S(2)}, u32[]{:S(2)}) %collective-permute-start.13) | collective-permute-done | bytes 98336 | tf_op jit(solution)/shard_map/ppermute | solution.py:16
  135.7 6.7 %collective-permute-done.14 = bf16[96,512]{1,0:T(8,128)(2,1)S(1)} collective-permute-done((bf16[96,512]{1,0:T(8,128)(2,1)S(1)}, bf16[96,512]{1,0:T(8,128)(2,1)S(1)}, u32[]{:S(2)}, u32[]{:S(2)}) %collective-permute-start.14) | collective-permute-done | bytes 98336 | tf_op jit(solution)/shard_map/ppermute | solution.py:16
  142.5 0.0 reduce-scatter.5.cloned.1.call-done
  142.5 1.4 fusion.10
  144.0 0.1 multiply_reduce_fusion.2
  144.1 29.5 %psum.14 = f32[256]{0:T(256)S(1)} all-reduce(f32[256]{0:T(256)S(1)} %add.209), channel_id=1, replica_groups=mesh['grp'=2,'row'=16] {'row'}, use_global_device_ids=true, to_apply=%region_4.5 | all-reduce | flops 256 | bytes 2048 | tf_op jit(solution)/shard_map/psum | solution.py:53
  173.6 0.1 multiply_convert_fusion.1
  173.7 0.1 broadcast.29
  173.9 0.1 collective-permute-start.15
  173.9 0.1 cosine_bitcast_fusion.1
  174.1 8.6 %collective-permute-done.15 = bf16[96,512]{1,0:T(8,128)(2,1)S(1)} collective-permute-done((bf16[96,512]{1,0:T(8,128)(2,1)S(1)}, bf16[96,512]{1,0:T(8,128)(2,1)S(1)}, u32[]{:S(2)}, u32[]{:S(2)}) %collective-permute-start.15) | collective-permute-done | bytes 98336 | tf_op jit(solution)/shard_map/ppermute | solution.py:16
  182.7 8.8 %collective-permute-done.16 = bf16[96,512]{1,0:T(8,128)(2,1)S(1)} collective-permute-done((bf16[96,512]{1,0:T(8,128)(2,1)S(1)}, bf16[96,512]{1,0:T(8,128)(2,1)S(1)}, u32[]{:S(2)}, u32[]{:S(2)}) %collective-permute-start.16) | collective-permute-done | bytes 98336 | tf_op jit(solution)/shard_map/ppermute | solution.py:16
  191.5 9.0 %collective-permute-done.17 = bf16[96,512]{1,0:T(8,128)(2,1)S(1)} collective-permute-done((bf16[96,512]{1,0:T(8,128)(2,1)S(1)}, bf16[96,512]{1,0:T(8,128)(2,1)S(1)}, u32[]{:S(2)}, u32[]{:S(2)}) %collective-permute-start.17) | collective-permute-done | bytes 98336 | tf_op jit(solution)/shard_map/ppermute | solution.py:16
  200.6 9.0 %collective-permute-done.18 = bf16[96,512]{1,0:T(8,128)(2,1)S(1)} collective-permute-done((bf16[96,512]{1,0:T(8,128)(2,1)S(1)}, bf16[96,512]{1,0:T(8,128)(2,1)S(1)}, u32[]{:S(2)}, u32[]{:S(2)}) %collective-permute-start.18) | collective-permute-done | bytes 98336 | tf_op jit(solution)/shard_map/ppermute | solution.py:16
  209.6 9.0 %collective-permute-done.19 = bf16[96,512]{1,0:T(8,128)(2,1)S(1)} collective-permute-done((bf16[96,512]{1,0:T(8,128)(2,1)S(1)}, bf16[96,512]{1,0:T(8,128)(2,1)S(1)}, u32[]{:S(2)}, u32[]{:S(2)}) %collective-permute-start.19) | collective-permute-done | bytes 98336 | tf_op jit(solution)/shard_map/ppermute | solution.py:16
  218.7 6.8 %collective-permute-done.20 = bf16[96,512]{1,0:T(8,128)(2,1)S(1)} collective-permute-done((bf16[96,512]{1,0:T(8,128)(2,1)S(1)}, bf16[96,512]{1,0:T(8,128)(2,1)S(1)}, u32[]{:S(2)}, u32[]{:S(2)}) %collective-permute-start.20) | collective-permute-done | bytes 98336 | tf_op jit(solution)/shard_map/ppermute | solution.py:16
  225.5 6.7 %collective-permute-done.21 = bf16[96,512]{1,0:T(8,128)(2,1)S(1)} collective-permute-done((bf16[96,512]{1,0:T(8,128)(2,1)S(1)}, bf16[96,512]{1,0:T(8,128)(2,1)S(1)}, u32[]{:S(2)}, u32[]{:S(2)}) %collective-permute-start.21) | collective-permute-done | bytes 98336 | tf_op jit(solution)/shard_map/ppermute | solution.py:16
  232.2 6.7 %collective-permute-done.22 = bf16[96,512]{1,0:T(8,128)(2,1)S(1)} collective-permute-done((bf16[96,512]{1,0:T(8,128)(2,1)S(1)}, bf16[96,512]{1,0:T(8,128)(2,1)S(1)}, u32[]{:S(2)}, u32[]{:S(2)}) %collective-permute-start.22) | collective-permute-done | bytes 98336 | tf_op jit(solution)/shard_map/ppermute | solution.py:16
  239.0 8.8 %collective-permute-done.23 = bf16[96,512]{1,0:T(8,128)(2,1)S(1)} collective-permute-done((bf16[96,512]{1,0:T(8,128)(2,1)S(1)}, bf16[96,512]{1,0:T(8,128)(2,1)S(1)}, u32[]{:S(2)}, u32[]{:S(2)}) %collective-permute-start.23) | collective-permute-done | bytes 98336 | tf_op jit(solution)/shard_map/ppermute | solution.py:16
  247.8 9.0 %collective-permute-done.24 = bf16[96,512]{1,0:T(8,128)(2,1)S(1)} collective-permute-done((bf16[96,512]{1,0:T(8,128)(2,1)S(1)}, bf16[96,512]{1,0:T(8,128)(2,1)S(1)}, u32[]{:S(2)}, u32[]{:S(2)}) %collective-permute-start.24) | collective-permute-done | bytes 98336 | tf_op jit(solution)/shard_map/ppermute | solution.py:16
  256.8 7.2 %collective-permute-done.25 = bf16[96,512]{1,0:T(8,128)(2,1)S(1)} collective-permute-done((bf16[96,512]{1,0:T(8,128)(2,1)S(1)}, bf16[96,512]{1,0:T(8,128)(2,1)S(1)}, u32[]{:S(2)}, u32[]{:S(2)}) %collective-permute-start.25) | collective-permute-done | bytes 98336 | tf_op jit(solution)/shard_map/ppermute | solution.py:16
  264.0 6.7 %collective-permute-done.26 = bf16[96,512]{1,0:T(8,128)(2,1)S(1)} collective-permute-done((bf16[96,512]{1,0:T(8,128)(2,1)S(1)}, bf16[96,512]{1,0:T(8,128)(2,1)S(1)}, u32[]{:S(2)}, u32[]{:S(2)}) %collective-permute-start.26) | collective-permute-done | bytes 98336 | tf_op jit(solution)/shard_map/ppermute | solution.py:16
  270.8 6.7 %collective-permute-done.27 = bf16[96,512]{1,0:T(8,128)(2,1)S(1)} collective-permute-done((bf16[96,512]{1,0:T(8,128)(2,1)S(1)}, bf16[96,512]{1,0:T(8,128)(2,1)S(1)}, u32[]{:S(2)}, u32[]{:S(2)}) %collective-permute-start.27) | collective-permute-done | bytes 98336 | tf_op jit(solution)/shard_map/ppermute | solution.py:16
  277.5 6.7 %collective-permute-done.28 = bf16[96,512]{1,0:T(8,128)(2,1)S(1)} collective-permute-done((bf16[96,512]{1,0:T(8,128)(2,1)S(1)}, bf16[96,512]{1,0:T(8,128)(2,1)S(1)}, u32[]{:S(2)}, u32[]{:S(2)}) %collective-permute-start.28) | collective-permute-done | bytes 98336 | tf_op jit(solution)/shard_map/ppermute | solution.py:16
  284.2 6.7 %collective-permute-done.29 = bf16[96,512]{1,0:T(8,128)(2,1)S(1)} collective-permute-done((bf16[96,512]{1,0:T(8,128)(2,1)S(1)}, bf16[96,512]{1,0:T(8,128)(2,1)S(1)}, u32[]{:S(2)}, u32[]{:S(2)}) %collective-permute-start.29) | collective-permute-done | bytes 98336 | tf_op jit(solution)/shard_map/ppermute | solution.py:16
  291.0 0.0 reduce-scatter.3.cloned.1.call-done
  291.0 1.4 fusion.12
  292.5 0.1 multiply_reduce_fusion
  292.6 29.5 %psum.15 = f32[256]{0:T(256)S(1)} all-reduce(f32[256]{0:T(256)S(1)} %add.213), channel_id=1, replica_groups=mesh['grp'=2,'row'=16] {'row'}, use_global_device_ids=true, to_apply=%region_7.8 | all-reduce | flops 256 | bytes 2048 | tf_op jit(solution)/shard_map/psum | solution.py:53
  322.1 0.8 broadcast_multiply_fusion
  (65 shorter events, 0.5 us)
Async XLA Ops:
  7.2 135.3 %reduce-scatter.5.cloned.1.call-start = ((), (), s32[]{:S(2)}) async-start(), calls=%async_computation.3 | async-start | bytes 10027008 | tf_op jit(solution)/shard_map/reduce_scatter | solution.py:37
  15.5 275.6 %reduce-scatter.3.cloned.1.call-start = ((), (), s32[]{:S(2)}) async-start(), calls=%async_computation.2 | async-start | bytes 10027008 | tf_op jit(solution)/shard_map/reduce_scatter | solution.py:37
  23.7 0.8 copy-start
  23.7 0.8 copy-start.1
  23.7 1.3 copy-start.2
  23.7 1.3 copy-start.3
  24.5 7.8 %collective-permute-start = (bf16[96,512]{1,0:T(8,128)(2,1)S(1)}, bf16[96,512]{1,0:T(8,128)(2,1)S(1)}, u32[]{:S(2)}, u32[]{:S(2)}) collective-permute-start(bf16[96,512]{1,0:T(8,128)(2,1)S(1)} %constant_dynamic-update-slice_fusion.32), channel_id=1, source_target_pairs={{0,1},{1,2},{2,3},{3,4},{4,5},{5,6},{6,7},{7,8},{8,9},{9,10},{10,1... | collective-permute-start | bytes 294920 | tf_op jit(solution)/shard_map/ppermute | solution.py:16
  32.3 6.7 %collective-permute-start.1 = (bf16[96,512]{1,0:T(8,128)(2,1)S(1)}, bf16[96,512]{1,0:T(8,128)(2,1)S(1)}, u32[]{:S(2)}, u32[]{:S(2)}) collective-permute-start(bf16[96,512]{1,0:T(8,128)(2,1)S(1)} %collective-permute-done), channel_id=1, source_target_pairs={{0,1},{1,2},{2,3},{3,4},{4,5},{5,6},{6,7},{7,8},{8,9},{9,10},{10,1... | collective-permute-start | bytes 294920 | tf_op jit(solution)/shard_map/ppermute | solution.py:16
  39.0 6.7 %collective-permute-start.2 = (bf16[96,512]{1,0:T(8,128)(2,1)S(1)}, bf16[96,512]{1,0:T(8,128)(2,1)S(1)}, u32[]{:S(2)}, u32[]{:S(2)}) collective-permute-start(bf16[96,512]{1,0:T(8,128)(2,1)S(1)} %collective-permute-done.1), channel_id=1, source_target_pairs={{0,1},{1,2},{2,3},{3,4},{4,5},{5,6},{6,7},{7,8},{8,9},{9,10},{10,1... | collective-permute-start | bytes 294920 | tf_op jit(solution)/shard_map/ppermute | solution.py:16
  45.8 6.7 %collective-permute-start.3 = (bf16[96,512]{1,0:T(8,128)(2,1)S(1)}, bf16[96,512]{1,0:T(8,128)(2,1)S(1)}, u32[]{:S(2)}, u32[]{:S(2)}) collective-permute-start(bf16[96,512]{1,0:T(8,128)(2,1)S(1)} %collective-permute-done.2), channel_id=1, source_target_pairs={{0,1},{1,2},{2,3},{3,4},{4,5},{5,6},{6,7},{7,8},{8,9},{9,10},{10,1... | collective-permute-start | bytes 294920 | tf_op jit(solution)/shard_map/ppermute | solution.py:16
  52.5 8.8 %collective-permute-start.4 = (bf16[96,512]{1,0:T(8,128)(2,1)S(1)}, bf16[96,512]{1,0:T(8,128)(2,1)S(1)}, u32[]{:S(2)}, u32[]{:S(2)}) collective-permute-start(bf16[96,512]{1,0:T(8,128)(2,1)S(1)} %collective-permute-done.3), channel_id=1, source_target_pairs={{0,1},{1,2},{2,3},{3,4},{4,5},{5,6},{6,7},{7,8},{8,9},{9,10},{10,1... | collective-permute-start | bytes 294920 | tf_op jit(solution)/shard_map/ppermute | solution.py:16
  61.3 8.9 %collective-permute-start.5 = (bf16[96,512]{1,0:T(8,128)(2,1)S(1)}, bf16[96,512]{1,0:T(8,128)(2,1)S(1)}, u32[]{:S(2)}, u32[]{:S(2)}) collective-permute-start(bf16[96,512]{1,0:T(8,128)(2,1)S(1)} %collective-permute-done.4), channel_id=1, source_target_pairs={{0,1},{1,2},{2,3},{3,4},{4,5},{5,6},{6,7},{7,8},{8,9},{9,10},{10,1... | collective-permute-start | bytes 294920 | tf_op jit(solution)/shard_map/ppermute | solution.py:16
  70.2 9.0 %collective-permute-start.6 = (bf16[96,512]{1,0:T(8,128)(2,1)S(1)}, bf16[96,512]{1,0:T(8,128)(2,1)S(1)}, u32[]{:S(2)}, u32[]{:S(2)}) collective-permute-start(bf16[96,512]{1,0:T(8,128)(2,1)S(1)} %collective-permute-done.5), channel_id=1, source_target_pairs={{0,1},{1,2},{2,3},{3,4},{4,5},{5,6},{6,7},{7,8},{8,9},{9,10},{10,1... | collective-permute-start | bytes 294920 | tf_op jit(solution)/shard_map/ppermute | solution.py:16
  79.2 9.1 %collective-permute-start.7 = (bf16[96,512]{1,0:T(8,128)(2,1)S(1)}, bf16[96,512]{1,0:T(8,128)(2,1)S(1)}, u32[]{:S(2)}, u32[]{:S(2)}) collective-permute-start(bf16[96,512]{1,0:T(8,128)(2,1)S(1)} %collective-permute-done.6), channel_id=1, source_target_pairs={{0,1},{1,2},{2,3},{3,4},{4,5},{5,6},{6,7},{7,8},{8,9},{9,10},{10,1... | collective-permute-start | bytes 294920 | tf_op jit(solution)/shard_map/ppermute | solution.py:16
  88.3 9.0 %collective-permute-start.8 = (bf16[96,512]{1,0:T(8,128)(2,1)S(1)}, bf16[96,512]{1,0:T(8,128)(2,1)S(1)}, u32[]{:S(2)}, u32[]{:S(2)}) collective-permute-start(bf16[96,512]{1,0:T(8,128)(2,1)S(1)} %collective-permute-done.7), channel_id=1, source_target_pairs={{0,1},{1,2},{2,3},{3,4},{4,5},{5,6},{6,7},{7,8},{8,9},{9,10},{10,1... | collective-permute-start | bytes 294920 | tf_op jit(solution)/shard_map/ppermute | solution.py:16
  97.3 6.8 %collective-permute-start.9 = (bf16[96,512]{1,0:T(8,128)(2,1)S(1)}, bf16[96,512]{1,0:T(8,128)(2,1)S(1)}, u32[]{:S(2)}, u32[]{:S(2)}) collective-permute-start(bf16[96,512]{1,0:T(8,128)(2,1)S(1)} %collective-permute-done.8), channel_id=1, source_target_pairs={{0,1},{1,2},{2,3},{3,4},{4,5},{5,6},{6,7},{7,8},{8,9},{9,10},{10,1... | collective-permute-start | bytes 294920 | tf_op jit(solution)/shard_map/ppermute | solution.py:16
  104.1 6.7 %collective-permute-start.10 = (bf16[96,512]{1,0:T(8,128)(2,1)S(1)}, bf16[96,512]{1,0:T(8,128)(2,1)S(1)}, u32[]{:S(2)}, u32[]{:S(2)}) collective-permute-start(bf16[96,512]{1,0:T(8,128)(2,1)S(1)} %collective-permute-done.9), channel_id=1, source_target_pairs={{0,1},{1,2},{2,3},{3,4},{4,5},{5,6},{6,7},{7,8},{8,9},{9,10},{10,1... | collective-permute-start | bytes 294920 | tf_op jit(solution)/shard_map/ppermute | solution.py:16
  110.9 7.0 %collective-permute-start.11 = (bf16[96,512]{1,0:T(8,128)(2,1)S(1)}, bf16[96,512]{1,0:T(8,128)(2,1)S(1)}, u32[]{:S(2)}, u32[]{:S(2)}) collective-permute-start(bf16[96,512]{1,0:T(8,128)(2,1)S(1)} %collective-permute-done.10), channel_id=1, source_target_pairs={{0,1},{1,2},{2,3},{3,4},{4,5},{5,6},{6,7},{7,8},{8,9},{9,10},{10,1... | collective-permute-start | bytes 294920 | tf_op jit(solution)/shard_map/ppermute | solution.py:16
  117.8 8.9 %collective-permute-start.12 = (bf16[96,512]{1,0:T(8,128)(2,1)S(1)}, bf16[96,512]{1,0:T(8,128)(2,1)S(1)}, u32[]{:S(2)}, u32[]{:S(2)}) collective-permute-start(bf16[96,512]{1,0:T(8,128)(2,1)S(1)} %collective-permute-done.11), channel_id=1, source_target_pairs={{0,1},{1,2},{2,3},{3,4},{4,5},{5,6},{6,7},{7,8},{8,9},{9,10},{10,1... | collective-permute-start | bytes 294920 | tf_op jit(solution)/shard_map/ppermute | solution.py:16
  126.7 9.0 %collective-permute-start.13 = (bf16[96,512]{1,0:T(8,128)(2,1)S(1)}, bf16[96,512]{1,0:T(8,128)(2,1)S(1)}, u32[]{:S(2)}, u32[]{:S(2)}) collective-permute-start(bf16[96,512]{1,0:T(8,128)(2,1)S(1)} %collective-permute-done.12), channel_id=1, source_target_pairs={{0,1},{1,2},{2,3},{3,4},{4,5},{5,6},{6,7},{7,8},{8,9},{9,10},{10,1... | collective-permute-start | bytes 294920 | tf_op jit(solution)/shard_map/ppermute | solution.py:16
  135.7 6.7 %collective-permute-start.14 = (bf16[96,512]{1,0:T(8,128)(2,1)S(1)}, bf16[96,512]{1,0:T(8,128)(2,1)S(1)}, u32[]{:S(2)}, u32[]{:S(2)}) collective-permute-start(bf16[96,512]{1,0:T(8,128)(2,1)S(1)} %collective-permute-done.13), channel_id=1, source_target_pairs={{0,1},{1,2},{2,3},{3,4},{4,5},{5,6},{6,7},{7,8},{8,9},{9,10},{10,1... | collective-permute-start | bytes 294920 | tf_op jit(solution)/shard_map/ppermute | solution.py:16
  173.9 8.8 %collective-permute-start.15 = (bf16[96,512]{1,0:T(8,128)(2,1)S(1)}, bf16[96,512]{1,0:T(8,128)(2,1)S(1)}, u32[]{:S(2)}, u32[]{:S(2)}) collective-permute-start(bf16[96,512]{1,0:T(8,128)(2,1)S(1)} %get-tuple-element.10), channel_id=1, source_target_pairs={{0,1},{1,2},{2,3},{3,4},{4,5},{5,6},{6,7},{7,8},{8,9},{9,10},{10,1... | collective-permute-start | bytes 294920 | tf_op jit(solution)/shard_map/ppermute | solution.py:16
  182.7 8.8 %collective-permute-start.16 = (bf16[96,512]{1,0:T(8,128)(2,1)S(1)}, bf16[96,512]{1,0:T(8,128)(2,1)S(1)}, u32[]{:S(2)}, u32[]{:S(2)}) collective-permute-start(bf16[96,512]{1,0:T(8,128)(2,1)S(1)} %collective-permute-done.15), channel_id=1, source_target_pairs={{0,1},{1,2},{2,3},{3,4},{4,5},{5,6},{6,7},{7,8},{8,9},{9,10},{10,1... | collective-permute-start | bytes 294920 | tf_op jit(solution)/shard_map/ppermute | solution.py:16
  191.5 9.1 %collective-permute-start.17 = (bf16[96,512]{1,0:T(8,128)(2,1)S(1)}, bf16[96,512]{1,0:T(8,128)(2,1)S(1)}, u32[]{:S(2)}, u32[]{:S(2)}) collective-permute-start(bf16[96,512]{1,0:T(8,128)(2,1)S(1)} %collective-permute-done.16), channel_id=1, source_target_pairs={{0,1},{1,2},{2,3},{3,4},{4,5},{5,6},{6,7},{7,8},{8,9},{9,10},{10,1... | collective-permute-start | bytes 294920 | tf_op jit(solution)/shard_map/ppermute | solution.py:16
  200.6 9.0 %collective-permute-start.18 = (bf16[96,512]{1,0:T(8,128)(2,1)S(1)}, bf16[96,512]{1,0:T(8,128)(2,1)S(1)}, u32[]{:S(2)}, u32[]{:S(2)}) collective-permute-start(bf16[96,512]{1,0:T(8,128)(2,1)S(1)} %collective-permute-done.17), channel_id=1, source_target_pairs={{0,1},{1,2},{2,3},{3,4},{4,5},{5,6},{6,7},{7,8},{8,9},{9,10},{10,1... | collective-permute-start | bytes 294920 | tf_op jit(solution)/shard_map/ppermute | solution.py:16
  209.6 9.1 %collective-permute-start.19 = (bf16[96,512]{1,0:T(8,128)(2,1)S(1)}, bf16[96,512]{1,0:T(8,128)(2,1)S(1)}, u32[]{:S(2)}, u32[]{:S(2)}) collective-permute-start(bf16[96,512]{1,0:T(8,128)(2,1)S(1)} %collective-permute-done.18), channel_id=1, source_target_pairs={{0,1},{1,2},{2,3},{3,4},{4,5},{5,6},{6,7},{7,8},{8,9},{9,10},{10,1... | collective-permute-start | bytes 294920 | tf_op jit(solution)/shard_map/ppermute | solution.py:16
  218.6 6.8 %collective-permute-start.20 = (bf16[96,512]{1,0:T(8,128)(2,1)S(1)}, bf16[96,512]{1,0:T(8,128)(2,1)S(1)}, u32[]{:S(2)}, u32[]{:S(2)}) collective-permute-start(bf16[96,512]{1,0:T(8,128)(2,1)S(1)} %collective-permute-done.19), channel_id=1, source_target_pairs={{0,1},{1,2},{2,3},{3,4},{4,5},{5,6},{6,7},{7,8},{8,9},{9,10},{10,1... | collective-permute-start | bytes 294920 | tf_op jit(solution)/shard_map/ppermute | solution.py:16
  225.5 6.7 %collective-permute-start.21 = (bf16[96,512]{1,0:T(8,128)(2,1)S(1)}, bf16[96,512]{1,0:T(8,128)(2,1)S(1)}, u32[]{:S(2)}, u32[]{:S(2)}) collective-permute-start(bf16[96,512]{1,0:T(8,128)(2,1)S(1)} %collective-permute-done.20), channel_id=1, source_target_pairs={{0,1},{1,2},{2,3},{3,4},{4,5},{5,6},{6,7},{7,8},{8,9},{9,10},{10,1... | collective-permute-start | bytes 294920 | tf_op jit(solution)/shard_map/ppermute | solution.py:16
  232.2 6.7 %collective-permute-start.22 = (bf16[96,512]{1,0:T(8,128)(2,1)S(1)}, bf16[96,512]{1,0:T(8,128)(2,1)S(1)}, u32[]{:S(2)}, u32[]{:S(2)}) collective-permute-start(bf16[96,512]{1,0:T(8,128)(2,1)S(1)} %collective-permute-done.21), channel_id=1, source_target_pairs={{0,1},{1,2},{2,3},{3,4},{4,5},{5,6},{6,7},{7,8},{8,9},{9,10},{10,1... | collective-permute-start | bytes 294920 | tf_op jit(solution)/shard_map/ppermute | solution.py:16
  239.0 8.8 %collective-permute-start.23 = (bf16[96,512]{1,0:T(8,128)(2,1)S(1)}, bf16[96,512]{1,0:T(8,128)(2,1)S(1)}, u32[]{:S(2)}, u32[]{:S(2)}) collective-permute-start(bf16[96,512]{1,0:T(8,128)(2,1)S(1)} %collective-permute-done.22), channel_id=1, source_target_pairs={{0,1},{1,2},{2,3},{3,4},{4,5},{5,6},{6,7},{7,8},{8,9},{9,10},{10,1... | collective-permute-start | bytes 294920 | tf_op jit(solution)/shard_map/ppermute | solution.py:16
  247.8 9.0 %collective-permute-start.24 = (bf16[96,512]{1,0:T(8,128)(2,1)S(1)}, bf16[96,512]{1,0:T(8,128)(2,1)S(1)}, u32[]{:S(2)}, u32[]{:S(2)}) collective-permute-start(bf16[96,512]{1,0:T(8,128)(2,1)S(1)} %collective-permute-done.23), channel_id=1, source_target_pairs={{0,1},{1,2},{2,3},{3,4},{4,5},{5,6},{6,7},{7,8},{8,9},{9,10},{10,1... | collective-permute-start | bytes 294920 | tf_op jit(solution)/shard_map/ppermute | solution.py:16
  256.8 7.2 %collective-permute-start.25 = (bf16[96,512]{1,0:T(8,128)(2,1)S(1)}, bf16[96,512]{1,0:T(8,128)(2,1)S(1)}, u32[]{:S(2)}, u32[]{:S(2)}) collective-permute-start(bf16[96,512]{1,0:T(8,128)(2,1)S(1)} %collective-permute-done.24), channel_id=1, source_target_pairs={{0,1},{1,2},{2,3},{3,4},{4,5},{5,6},{6,7},{7,8},{8,9},{9,10},{10,1... | collective-permute-start | bytes 294920 | tf_op jit(solution)/shard_map/ppermute | solution.py:16
  264.0 6.7 %collective-permute-start.26 = (bf16[96,512]{1,0:T(8,128)(2,1)S(1)}, bf16[96,512]{1,0:T(8,128)(2,1)S(1)}, u32[]{:S(2)}, u32[]{:S(2)}) collective-permute-start(bf16[96,512]{1,0:T(8,128)(2,1)S(1)} %collective-permute-done.25), channel_id=1, source_target_pairs={{0,1},{1,2},{2,3},{3,4},{4,5},{5,6},{6,7},{7,8},{8,9},{9,10},{10,1... | collective-permute-start | bytes 294920 | tf_op jit(solution)/shard_map/ppermute | solution.py:16
  270.8 6.7 %collective-permute-start.27 = (bf16[96,512]{1,0:T(8,128)(2,1)S(1)}, bf16[96,512]{1,0:T(8,128)(2,1)S(1)}, u32[]{:S(2)}, u32[]{:S(2)}) collective-permute-start(bf16[96,512]{1,0:T(8,128)(2,1)S(1)} %collective-permute-done.26), channel_id=1, source_target_pairs={{0,1},{1,2},{2,3},{3,4},{4,5},{5,6},{6,7},{7,8},{8,9},{9,10},{10,1... | collective-permute-start | bytes 294920 | tf_op jit(solution)/shard_map/ppermute | solution.py:16
  277.5 6.7 %collective-permute-start.28 = (bf16[96,512]{1,0:T(8,128)(2,1)S(1)}, bf16[96,512]{1,0:T(8,128)(2,1)S(1)}, u32[]{:S(2)}, u32[]{:S(2)}) collective-permute-start(bf16[96,512]{1,0:T(8,128)(2,1)S(1)} %collective-permute-done.27), channel_id=1, source_target_pairs={{0,1},{1,2},{2,3},{3,4},{4,5},{5,6},{6,7},{7,8},{8,9},{9,10},{10,1... | collective-permute-start | bytes 294920 | tf_op jit(solution)/shard_map/ppermute | solution.py:16
  284.2 6.7 %collective-permute-start.29 = (bf16[96,512]{1,0:T(8,128)(2,1)S(1)}, bf16[96,512]{1,0:T(8,128)(2,1)S(1)}, u32[]{:S(2)}, u32[]{:S(2)}) collective-permute-start(bf16[96,512]{1,0:T(8,128)(2,1)S(1)} %collective-permute-done.28), channel_id=1, source_target_pairs={{0,1},{1,2},{2,3},{3,4},{4,5},{5,6},{6,7},{7,8},{8,9},{9,10},{10,1... | collective-permute-start | bytes 294920 | tf_op jit(solution)/shard_map/ppermute | solution.py:16
Sparse Core Ops, SparseCore 0:
  15.6 119.8 reduce-scatter.4
  140.1 119.2 reduce-scatter.2
